TPU v7x, 512 devices: a whole 4x8x8 slice. The times are simulated.
512 devices in a mesh: dp: 8 (over z), cent: 64 (over x, y, core).
Axes of the slice: x: 4, y: 8, z: 8, core: 2. Of those that a mesh axis runs over, the one named last changes fastest.
Arguments:
- points: bfloat16 [24576, 1024], P(('dp', 'cent')), may hold values from -6 to 6
- assign: int32 [24576], P(('dp', 'cent')), may hold values from 0 to 32767, as said below
- centroids: float32 [32768, 1024], P('cent'), may hold values from -6 to 6
- counts: int32 [32768], P('cent'), may hold values from 1 to 4
Outputs:
- new_centroids: float32 [32768, 1024], P('cent')
- best: float32 [24576], P(('dp', 'cent'))
Inputs may be any that keep to these rules, and one draw needn't show every extreme that they name: `assign`: split the points into aligned blocks of 3072 points in order (the points of one dp index). In every block, the clusters k * 512 to (k + 1) * 512 - 1 receive exactly 48 points together, for every k.
All inputs are finite; a program needn't handle non-finite values.
Results may differ from a plain program's by a relative error of at most 0.0003.
Values may be sent and summed in bfloat16 or wider, within the bound.
No kernel may reach another device: no remote copies, remote signals or barrier semaphores. Data moves between devices by JAX's collectives and lax.ppermute only.
A program may use at most 128 MiB of HBM per device.

v0:
```python
import jax
import jax.numpy as jnp
from jax import lax
from jax.sharding import PartitionSpec as P


def renorm(merged):
    return merged * lax.rsqrt(jnp.mean(merged * merged, axis=1, keepdims=True) + 1e-05)


def cluster_terms(rows, labels, kdev):
    first = lax.axis_index("cent") * kdev
    local = labels - first
    onehot = (local[None, :] == jnp.arange(kdev, dtype=jnp.int32)[:, None]).astype(jnp.bfloat16)
    return jnp.dot(onehot, rows, preferred_element_type=jnp.float32)


def per_device(points, assign, centroids, counts):
    kdev = centroids.shape[0]
    pdev = points.shape[0]
    weighted = centroids * counts.astype(jnp.float32)[:, None]
    rows, labels = (
        lax.all_gather(points, "cent", axis=0, tiled=True),
        lax.all_gather(assign, "cent", axis=0, tiled=True),
    )
    sums = cluster_terms(rows, labels, kdev)
    total = lax.psum(sums, "dp")
    fresh = renorm(weighted + total)
    rounded = fresh.astype(jnp.bfloat16)
    scores = jnp.dot(rows, rounded.T, preferred_element_type=jnp.float32)
    local_best = jnp.max(scores, axis=1)
    merged_best = lax.pmax(local_best, "cent")
    top = lax.dynamic_slice_in_dim(merged_best, lax.axis_index("cent") * pdev, pdev, 0)
    values = points.astype(jnp.float32)
    width = points.shape[1]
    scale = width * jnp.sqrt(jnp.mean(values * values, axis=1) + 1e-06)
    return (fresh, top / scale)


def solution(mesh):
    placed = (P(("dp", "cent"), None), P(("dp", "cent")), P("cent", None), P("cent"))
    return jax.shard_map(
        per_device,
        mesh=mesh,
        in_specs=placed,
        out_specs=(P("cent", None), P(("dp", "cent"))),
        check_vma=False,
    )
```

profile of v0, /device:TPU:64, one launch (start us, length us, event | category | flops | bytes accessed | tf_op | source)
XLA Modules:
  0.0 617.8 jit_solution(2940238520247544569)
XLA Ops:
  7.2 0.0 all-gather.2.cloned.1.call-start
  7.2 0.7 all-gather.2.cloned.1.call-update
  7.9 0.0 all-reduce.3.cloned.1.call-start
  7.9 1.3 dynamic-slice
  9.9 0.9 dynamic-update-slice
  10.8 251.6 %all-reduce = s32[3072]{0:T(1024)S(1)} all-reduce(s32[3072]{0:T(1024)S(1)} %dynamic-update-slice), channel_id=1, replica_groups=mesh['dp'=8,'cent'=64] {'cent'}, use_global_device_ids=true, to_apply=%add | all-reduce | flops 3072 | bytes 24576
  262.4 0.0 all-gather.2.cloned.1.call-done
  262.4 0.0 copy-start.3
  262.4 7.5 %fusion = f32[512,1024]{1,0:T(8,128)} fusion(bf16[3072,1024]{1,0:T(8,128)(2,1)} %all-gather.2.cloned.1.call-done, s32[3072]{0:T(1024)S(1)} %broadcast_subtract_fusion), kind=kOutput, calls=%fused_computation.1 | convolution fusion | flops 3222798336 | bytes 8400896 | tf_op jit(solution)/shard_map/dot_general | solution.py:15
  269.9 0.0 copy-start.4
  269.9 0.0 copy-start
  269.9 0.0 all-reduce.3.cloned.1.call-update
  269.9 0.7 copy-done.4
  270.6 0.0 copy-done.3
  270.6 0.1 multiply_reduce_fusion.1
  270.7 83.2 %all-reduce.3.cloned.1.call-done = f32[512,1024]{1,0:T(8,128)} async-done(((f32[512,1024]{1,0:T(8,128)}), f32[512,1024]{1,0:T(8,128)}) %all-reduce.3.cloned.1.call-update) | async-done | bytes 2097168 | tf_op jit(solution)/shard_map/psum | solution.py:27
  353.9 0.0 copy-done
  353.9 0.0 copy-start.1
  353.9 2.2 multiply_reduce_fusion
  356.1 0.1 copy-done.1
  356.1 0.0 copy-start.5
  356.1 0.4 broadcast_multiply_fusion
  356.5 0.0 copy-start.2
  356.5 1.3 copy-done.2
  357.8 1.8 copy-done.5
  359.7 3.7 convolution_reduce_fusion
  363.4 247.0 %pmax.7 = f32[3072]{0:T(1024)S(1)} all-reduce(f32[3072]{0:T(1024)S(1)} %convolution_reduce_fusion), channel_id=1, replica_groups=mesh['dp'=8,'cent'=64] {'cent'}, use_global_device_ids=true, to_apply=%region_3.0 | all-reduce | flops 3072 | bytes 24576 | tf_op jit(solution)/shard_map/pmax | solution.py:32
  610.4 0.6 multiply_divide_fusion
  (4 shorter events, 0.0 us)
Async XLA Ops:
  7.2 255.2 %all-gather.2.cloned.1.call-start = ((), (), s32[]{:S(2)}) async-start(), calls=%async_computation | async-start | bytes 6389760 | tf_op jit(solution)/shard_map/all_gather | solution.py:23
  7.9 346.0 %all-reduce.3.cloned.1.call-start = ((), (), s32[]{:S(2)}) async-start(), calls=%async_computation.1 | async-start | bytes 4194304 | tf_op jit(solution)/shard_map/psum | solution.py:27
  262.4 8.2 %copy-start.3 = (bf16[48,1024]{1,0:T(8,128)(2,1)S(1)}, bf16[48,1024]{1,0:T(8,128)(2,1)}, u32[]{:S(2)}) copy-start(bf16[48,1024]{1,0:T(8,128)(2,1)} %param.4) | copy-start | bytes 294916
  269.9 0.7 copy-start.4
  269.9 84.0 %copy-start = (f32[512,1024]{1,0:T(8,128)S(1)}, f32[512,1024]{1,0:T(8,128)}, u32[]{:S(2)}) copy-start(f32[512,1024]{1,0:T(8,128)} %param.6) | copy-start | bytes 6291460
  353.9 2.2 copy-start.1
  356.1 3.5 copy-start.5
  356.5 1.3 copy-start.2
Sparse Core Ops, SparseCore 0:
  11.3 89.7 all-gather.1
  270.1 83.7 all-reduce.2
where the time goes:
time: 618 us
  blocking collectives  499 us (81%)
  waiting for transfers between devices  83.9 us (14%)
  between operations  14.7 us (2%)
  matrix products  11.3 us (2%)
    unnamed x1, blocking collectives  252 us
    pmax x1, blocking collectives, per_device(): merged_best = lax.pmax(local_best, 'cent')  247 us
    psum x1, waiting for transfers between devices, per_device(): total = lax.psum(sums, 'dp')  83.2 us
  transfers between devices with their start and end apart: 2, of which 1 were waited for; matrix products, arithmetic and copies ran while one was open for 0% of the time, Pallas kernels for 0%

commit v1 on v0

--- a/solution.py
+++ b/solution.py
@@ -24,7 +24,7 @@
         lax.all_gather(assign, "cent", axis=0, tiled=True),
     )
     sums = cluster_terms(rows, labels, kdev)
-    total = lax.psum(sums, "dp")
+    total = jnp.sum(lax.all_gather(sums, "dp"), axis=0)
     fresh = renorm(weighted + total)
     rounded = fresh.astype(jnp.bfloat16)
     scores = jnp.dot(rows, rounded.T, preferred_element_type=jnp.float32)

time: 618 us -> 717 us (1.16)
  waiting for transfers between devices: 83.9 us -> 170 us
  other arithmetic: 3.25 us -> 11.4 us
    all_gather x0 -> x1, waiting for transfers between devices: none -> 169 us  [per_device(): total = jnp.sum(lax.all_gather(sums, 'dp'), axis=0)]
    psum x1 -> x0, waiting for transfers between devices: 83.2 us -> none  [per_device(): total = lax.psum(sums, 'dp')]
    reduce_sum x0 -> x1, other arithmetic: none -> 8.06 us  [per_device(): total = jnp.sum(lax.all_gather(sums, 'dp'), axis=0)]
where the time goes in v1:
time: 717 us
  blocking collectives  502 us (70%)
  waiting for transfers between devices  170 us (24%)
  between operations  14.8 us (2%)
  matrix products  14 us (2%)
  other arithmetic  11.4 us (2%)
    unnamed x1, blocking collectives  252 us
    pmax x1, blocking collectives, per_device(): merged_best = lax.pmax(local_best, 'cent')  250 us
    all_gather x1, waiting for transfers between devices, per_device(): total = jnp.sum(lax.all_gather(sums, 'dp'), axis=0)  169 us
  transfers between devices with their start and end apart: 2, of which 1 were waited for; matrix products, arithmetic and copies ran while one was open for 0% of the time, Pallas kernels for 0%

profile of v1, /device:TPU:64, one launch (start us, length us, event | category | flops | bytes accessed | tf_op | source)
XLA Modules:
  0.0 716.5 jit_solution(1433299862973145970)
XLA Ops:
  7.2 0.0 all-gather.4.cloned.1.call-start
  7.2 0.7 all-gather.4.cloned.1.call-update
  7.9 0.0 all-gather.6.cloned.1.call-start
  7.9 1.3 dynamic-slice
  9.9 0.9 dynamic-update-slice
  10.8 251.7 %all-reduce = s32[3072]{0:T(1024)S(1)} all-reduce(s32[3072]{0:T(1024)S(1)} %dynamic-update-slice), channel_id=1, replica_groups=mesh['dp'=8,'cent'=64] {'cent'}, use_global_device_ids=true, to_apply=%add | all-reduce | flops 3072 | bytes 24576
  262.4 0.0 all-gather.4.cloned.1.call-done
  262.4 7.5 %fusion = f32[512,1024]{1,0:T(8,128)} fusion(bf16[3072,1024]{1,0:T(8,128)(2,1)} %all-gather.4.cloned.1.call-done, s32[3072]{0:T(1024)S(1)} %broadcast_subtract_fusion), kind=kOutput, calls=%fused_computation.1 | convolution fusion | flops 3222798336 | bytes 8400896 | tf_op jit(solution)/shard_map/dot_general | solution.py:15
  269.9 0.0 copy-start.3
  269.9 0.0 copy-start.2
  269.9 0.0 all-gather.6.cloned.1.call-update
  270.0 0.7 copy-done.3
  270.6 0.2 copy-done.2
  270.8 0.1 multiply_reduce_fusion.1
  271.0 169.3 %all-gather.6.cloned.1.call-done = f32[4096,1024]{1,0:T(8,128)} async-done(((f32[512,1024]{1,0:T(8,128)}), f32[4096,1024]{1,0:T(8,128)}) %all-gather.6.cloned.1.call-update) | async-done | bytes 16777232 | tf_op jit(solution)/shard_map/all_gather | solution.py:27
  440.2 8.1 %reduce_sum.27 = f32[512,1024]{1,0:T(8,128)S(1)} reduce(f32[8,512,1024]{2,1,0:T(8,128)} %bitcast.4, f32[]{:T(128)} %constant.4.clone.1), dimensions={0}, to_apply=%region_0.0 | reduce | flops 3670016 | bytes 18874372 | tf_op jit(solution)/shard_map/reduce_sum | solution.py:27
  448.3 0.0 copy-start
  448.3 2.2 multiply_reduce_fusion
  450.5 0.0 copy-done
  450.5 0.4 broadcast_multiply_fusion
  450.9 0.0 copy-start.1
  450.9 1.3 copy-done.1
  452.3 6.5 convolution_reduce_fusion
  458.8 250.3 %pmax.7 = f32[3072]{0:T(1024)S(1)} all-reduce(f32[3072]{0:T(1024)S(1)} %convolution_reduce_fusion), channel_id=1, replica_groups=mesh['dp'=8,'cent'=64] {'cent'}, use_global_device_ids=true, to_apply=%region_3.0 | all-reduce | flops 3072 | bytes 24576 | tf_op jit(solution)/shard_map/pmax | solution.py:32
  709.1 0.6 multiply_divide_fusion
  (4 shorter events, 0.0 us)
Async XLA Ops:
  7.2 255.2 %all-gather.4.cloned.1.call-start = ((), (), s32[]{:S(2)}) async-start(), calls=%async_computation | async-start | bytes 6389760 | tf_op jit(solution)/shard_map/all_gather | solution.py:23
  7.9 432.3 %all-gather.6.cloned.1.call-start = ((), (), s32[]{:S(2)}) async-start(), calls=%async_computation.1 | async-start | bytes 18874368 | tf_op jit(solution)/shard_map/all_gather | solution.py:27
  269.9 0.7 copy-start.3
  269.9 0.9 copy-start.2
  448.3 2.2 copy-start
  450.9 1.3 copy-start.1
Sparse Core Ops, SparseCore 0:
  11.3 89.7 all-gather.3
  270.1 170.1 all-gather.5
